TPU v7x, 128 devices: a whole 4x4x4 slice. The times are simulated.
128 devices in a mesh: src: 16 (over x_lo, z, core), loop: 8 (over x_hi, y).
Axes of the slice: x: 4 (x_hi: 2, x_lo: 2; x = x_hi * 2 + x_lo), y: 4, z: 4, core: 2. Of those that a mesh axis runs over, the one named last changes fastest.
Arguments:
- sources: bfloat16 [65536, 768], P(('src', 'loop')), may hold values from -48 to 48
- log_a: float32 [65536], P(('src', 'loop')), may hold values from -3 to 0
- targets: bfloat16 [128, 512, 768], P('src'), may hold values from -6 to 6
- g_old: bfloat16 [128, 512], P('src'), may hold values from -2.5 to 2.5
- log_b: float32 [128, 512], P('src'), may hold values from -3 to 0
- tile_ids: int32 [128, 16, 2], P(('src', 'loop')), may hold values from 0 to 127, as said below
- live_count: int32 [128, 16], P(('src', 'loop')), may hold values from 1 to 2, as said below
Outputs:
- f_new: float32 [65536], P(('src', 'loop'))
- g_new: float32 [128, 512], P('src')
Inputs may be any that keep to these rules, and one draw needn't show every extreme that they name: `tile_ids`: tile ids of one device for index o of src lie in o * 8 to (o + 1) * 8 - 1 and are distinct within that group of 2 slots; every tile is in use in some device's list. `live_count`: every index of src has a full group of 2 slots in use in some device's list.
All inputs are finite; a program needn't handle non-finite values.
Results may differ from a plain program's by a relative error of at most 0.0003.
Values may be sent and summed in bfloat16 or wider, within the bound.
No kernel may reach another device: no remote copies, remote signals or barrier semaphores. Data moves between devices by JAX's collectives and lax.ppermute only.
A program may use at most 128 MiB of HBM per device.

v0:
```python
import math
import jax
import jax.numpy as jnp
from jax import lax
from jax.sharding import PartitionSpec as P

EPSILON = 0.1
VERY_LOW = -1e30


def similarity(rows_bf, fetched):
    kernel = jnp.einsum("rd,ctd->rct", rows_bf, fetched, preferred_element_type=jnp.float32)
    return kernel / math.sqrt(rows_bf.shape[1])


def row_part(rows_bf, fetched, potential, live_slots):
    kernel = similarity(rows_bf, fetched)
    logits = (potential.astype(jnp.float32)[None] + kernel) / EPSILON
    logits = jnp.where(live_slots[None, :, None], logits, VERY_LOW)
    top = jnp.max(logits, axis=(1, 2))
    total = jnp.sum(jnp.exp(logits - top[:, None, None]), axis=(1, 2))
    return (top, total)


def col_part(rows_bf, row_potential, fetched, live_slots):
    kernel = similarity(rows_bf, fetched)
    logits = (row_potential[:, None, None] + kernel) / EPSILON
    top = jnp.max(logits, axis=0)
    total = jnp.sum(jnp.exp(logits - top[None]), axis=0)
    top = jnp.where(live_slots[:, None], top, VERY_LOW)
    total = jnp.where(live_slots[:, None], total, 0.0)
    return (top, total)


def local(sources, log_a, targets, g_old, log_b, tile_ids, live_count):
    tiles_own = targets.shape[0]
    width = targets.shape[1]
    slots_per = tile_ids.shape[2]
    me = lax.axis_index("src")
    rows_all = lax.all_gather(sources, "src")
    log_a_all = lax.all_gather(log_a, "src")
    ids_all = lax.all_gather(tile_ids[0], "src")
    live_all = lax.all_gather(live_count[0], "src")
    my_ids = lax.dynamic_index_in_dim(ids_all, me, 1, False) - me * tiles_own
    my_count = lax.dynamic_index_in_dim(live_all, me, 1, False)
    live_slots = jnp.arange(slots_per, dtype=jnp.int32)[None, :] < my_count[:, None]

    def rows_of(item):
        rows_bf, ids, live = item
        return row_part(rows_bf, targets[ids], g_old[ids], live)

    row_top, row_total = lax.map(rows_of, (rows_all, my_ids, live_slots))
    top = lax.pmax(row_top, "src")
    total = lax.psum(row_total * jnp.exp(row_top - top), "src")
    f_all = EPSILON * log_a_all - EPSILON * (top + jnp.log(total))
    f_new = lax.dynamic_index_in_dim(f_all, me, 0, False)

    def cols_of(item):
        rows_bf, f_rows, ids, live = item
        return col_part(rows_bf, f_rows, targets[ids], live)

    col_top, col_total = lax.map(cols_of, (rows_all, f_all, my_ids, live_slots))
    flat_ids = my_ids.reshape(-1)
    flat_top = col_top.reshape(-1, width)
    flat_total = col_total.reshape(-1, width)
    onehot = flat_ids[:, None] == jnp.arange(tiles_own, dtype=jnp.int32)[None, :]
    tile_top = jnp.max(jnp.where(onehot[:, :, None], flat_top[:, None, :], VERY_LOW), axis=0)
    scaled = flat_total[:, None, :] * jnp.exp(
        jnp.minimum(flat_top[:, None, :] - tile_top[None], 0.0)
    )
    tile_total = jnp.sum(jnp.where(onehot[:, :, None], scaled, 0.0), axis=0)
    all_top = lax.pmax(tile_top, "loop")
    all_total = lax.psum(tile_total * jnp.exp(tile_top - all_top), "loop")
    g_new = EPSILON * log_b - EPSILON * (all_top + jnp.log(all_total))
    return (f_new, g_new)


def solution(mesh):
    return jax.shard_map(
        local,
        mesh=mesh,
        in_specs=(
            P(("src", "loop"), None),
            P(("src", "loop")),
            P("src", None, None),
            P("src", None),
            P("src", None),
            P(("src", "loop"), None, None),
            P(("src", "loop"), None),
        ),
        out_specs=(P(("src", "loop")), P("src", None)),
        check_vma=False,
    )
```

profile of v0, /device:TPU:0, one launch (start us, length us, event | category | flops | bytes accessed | tf_op | source)
XLA Modules:
  0.0 501.2 jit_solution(8894537044187313514)
XLA Ops:
  7.9 21.4 %all_gather.21 = s32[16,16,2]{1,2,0:T(2,128)S(1)} all-gather(s32[1,16,2]{1,2,0:T(2,128)} %param.16), channel_id=1, replica_groups=mesh['src'=16,'loop'=8] {'src'}, dimensions={0}, use_global_device_ids=true | all-gather | bytes 2176 | tf_op jit(solution)/shard_map/all_gather | solution.py:42
  30.1 17.0 %all-gather.3 = s32[16,1,16]{2,1,0:T(1,128)S(1)} all-gather(s32[1,1,16]{2,1,0:T(1,128)} %bitcast.87), channel_id=1, replica_groups=mesh['src'=16,'loop'=8] {'src'}, dimensions={0}, use_global_device_ids=true | all-gather | bytes 1088 | tf_op jit(solution)/shard_map/all_gather | solution.py:43
  47.5 18.6 %all-gather.2 = f32[16,1,512]{2,1,0:T(1,128)S(1)} all-gather(f32[1,1,512]{2,1,0:T(1,128)} %bitcast.85), channel_id=2, replica_groups=mesh['src'=16,'loop'=8] {'src'}, dimensions={0}, use_global_device_ids=true | all-gather | bytes 34816 | tf_op jit(solution)/shard_map/all_gather | solution.py:41
  66.2 18.0 %all-gather.6.cloned.1.call-done = bf16[8192,768]{1,0:T(8,128)(2,1)} async-done(((bf16[512,768]{1,0:T(8,128)(2,1)}), bf16[8192,768]{1,0:T(8,128)(2,1)}) %all-gather.6.cloned.1.call-update) | async-done | bytes 12582928 | tf_op jit(solution)/shard_map/all_gather | solution.py:40
  84.2 120.7 %while.24 = (s32[]{:T(128)}, f32[16,512]{1,0:T(8,128)S(1)}, f32[16,512]{1,0:T(8,128)S(1)}, pred[16,2]{1,0:T(8,128)(4,1)S(1)}, s32[16,2]{1,0:T(8,128)S(1)}, /*ind...) while((s32[]{:T(128)}, f32[16,512]{1,0:T(8,128)S(1)}, ...), condition=%wide.region_3.4_spmd, body=%wide.region_0.3_spmd.sunk | while | flops 808977408 | bytes 9732271 | solution.py:52
  85.5 3.4 gather_fusion
  93.1 3.4 gather_fusion
  100.6 3.4 gather_fusion
  108.1 3.4 gather_fusion
  115.7 3.4 gather_fusion
  123.2 3.4 gather_fusion
  130.8 3.4 gather_fusion
  138.3 3.4 gather_fusion
  145.9 3.4 gather_fusion
  153.4 3.4 gather_fusion
  161.0 3.4 gather_fusion
  168.5 3.4 gather_fusion
  176.1 3.4 gather_fusion
  204.9 55.7 %pmax.14 = f32[16,512]{1,0:T(8,128)S(1)} all-reduce(f32[16,512]{1,0:T(8,128)S(1)} %get-tuple-element.88), channel_id=1, replica_groups=mesh['src'=16,'loop'=8] {'src'}, use_global_device_ids=true, to_apply=%region_4.5 | all-reduce | flops 8192 | bytes 65536 | tf_op jit(solution)/shard_map/pmax | solution.py:53
  260.7 52.9 %psum.14 = f32[16,512]{1,0:T(8,128)S(1)} all-reduce(f32[16,512]{1,0:T(8,128)S(1)} %exponential_multiply_fusion), channel_id=1, replica_groups=mesh['src'=16,'loop'=8] {'src'}, use_global_device_ids=true, to_apply=%region_5.6 | all-reduce | flops 8192 | bytes 65536 | tf_op jit(solution)/shard_map/psum | solution.py:54
  314.2 101.2 %while.25 = (s32[]{:T(128)}, f32[16,2,512]{2,1,0:T(2,128)S(1)}, f32[16,2,512]{2,1,0:T(2,128)S(1)}, pred[16,2]{1,0:T(8,128)(4,1)S(1)}, f32[16,512]{1,0:T(8,128)S(...) while((s32[]{:T(128)}, f32[16,2,512]{2,1,0:T(2,128)S(1)}, ...), condition=%wide.region_9.10_spmd, body=%wide.region_6.9_spmd.sunk | while | flops 810025984 | bytes 9740957 | solution.py:62
  314.2 3.4 gather_fusion.2
  320.6 3.4 gather_fusion.2
  326.9 3.4 gather_fusion.2
  339.5 3.4 gather_fusion.2
  352.2 3.4 gather_fusion.2
  364.8 3.4 gather_fusion.2
  377.5 3.4 gather_fusion.2
  390.1 3.4 gather_fusion.2
  402.8 3.4 gather_fusion.2
  415.6 41.4 %pmax.15 = f32[8,512]{1,0:T(8,128)S(1)} all-reduce(f32[8,512]{1,0:T(8,128)S(1)} %select_reduce_fusion.1), channel_id=1, replica_groups=mesh['src'=16,'loop'=8] {'loop'}, use_global_device_ids=true, to_apply=%region_11.12 | all-reduce | flops 4096 | bytes 32768 | tf_op jit(solution)/shard_map/pmax | solution.py:72
  457.1 36.6 %psum.15 = f32[8,512]{1,0:T(8,128)S(1)} all-reduce(f32[8,512]{1,0:T(8,128)S(1)} %exponential_multiply_fusion.1), channel_id=1, replica_groups=mesh['src'=16,'loop'=8] {'loop'}, use_global_device_ids=true, to_apply=%region_13.14 | all-reduce | flops 4096 | bytes 32768 | tf_op jit(solution)/shard_map/psum | solution.py:73
  (291 shorter events, 148.3 us)
Async XLA Ops:
  7.2 77.0 %all-gather.6.cloned.1.call-start = ((), (), s32[]{:S(2)}) async-start(), calls=%async_computation | async-start | bytes 13369344 | tf_op jit(solution)/shard_map/all_gather | solution.py:40
  314.2 179.6 %copy-start = (f32[8,512]{1,0:T(8,128)S(1)}, f32[8,512]{1,0:T(8,128)}, u32[]{:S(2)}) copy-start(f32[8,512]{1,0:T(8,128)} %param.15) | copy-start | bytes 49156
Sparse Core Ops, SparseCore 0:
  9.7 74.4 all-gather.5
where the time goes:
time: 505 us; the launch traced here: 501 us
  blocking collectives  244 us (48%)
  local copies, waits for them, and re-layouts  134 us (27%)
  matrix products  70.9 us (14%)
  waiting for transfers between devices  18.7 us (4%)
  other arithmetic  18.2 us (4%)
  between operations  14.1 us (3%)
    gather x32, local copies, waits for them, and re-layouts, rows_of(): return row_part(rows_bf, targets[ids], g_old[ids], live)  75.1 us
    dot_general x32, matrix products, similarity(): jnp.einsum('rd,ctd->rct', rows_bf, fetched, preferred_element_type=jnp.fl...  70.9 us
    pmax x1, blocking collectives, local(): top = lax.pmax(row_top, 'src')  55.7 us
    gather x16, local copies, waits for them, and re-layouts, cols_of(): return col_part(rows_bf, f_rows, targets[ids], live)  54.9 us
    psum x1, blocking collectives, local(): total = lax.psum(row_total * jnp.exp(row_top - top), 'src')  52.9 us
    pmax x1, blocking collectives, local(): all_top = lax.pmax(tile_top, 'loop')  41.4 us
    psum x1, blocking collectives, local(): all_total = lax.psum(tile_total * jnp.exp(tile_top - all_top), 'loop')  36.6 us
    all_gather x1, blocking collectives, local(): ids_all = lax.all_gather(tile_ids[0], 'src')  21.4 us
  transfers between devices with their start and end apart: 1, of which 1 were waited for; matrix products, arithmetic and copies ran while one was open for 0% of the time, Pallas kernels for 0%

commit v1 on v0

--- a/solution.py
+++ b/solution.py
@@ -6,6 +6,10 @@
 
 EPSILON = 0.1
 VERY_LOW = -1e30
+
+
+def plan_the_pairs_all(block_in):
+    return jnp.sum(lax.all_gather(block_in, "loop"), axis=0)
 
 
 def similarity(rows_bf, fetched):
@@ -70,7 +74,7 @@
     )
     tile_total = jnp.sum(jnp.where(onehot[:, :, None], scaled, 0.0), axis=0)
     all_top = lax.pmax(tile_top, "loop")
-    all_total = lax.psum(tile_total * jnp.exp(tile_top - all_top), "loop")
+    all_total = plan_the_pairs_all(tile_total * jnp.exp(tile_top - all_top))
     g_new = EPSILON * log_b - EPSILON * (all_top + jnp.log(all_total))
     return (f_new, g_new)
 

time: 505 us -> 502 us (level)
    psum x1 -> x0, blocking collectives: 36.6 us -> none  [local(): all_total = lax.psum(tile_total * jnp.exp(tile_top - all_top), 'loop')]
    all_gather x0 -> x1, blocking collectives: none -> 34.2 us  [plan_the_pairs_all(): return jnp.sum(lax.all_gather(block_in, 'loop'), axis=0)]
where the time goes in v1:
time: 502 us; the launch traced here: 499 us
  blocking collectives  241 us (48%)
  local copies, waits for them, and re-layouts  134 us (27%)
  matrix products  70.9 us (14%)
  waiting for transfers between devices  18.7 us (4%)
  other arithmetic  18.2 us (4%)
  between operations  14.1 us (3%)
    gather x32, local copies, waits for them, and re-layouts, rows_of(): return row_part(rows_bf, targets[ids], g_old[ids], live)  75.1 us
    dot_general x32, matrix products, similarity(): jnp.einsum('rd,ctd->rct', rows_bf, fetched, preferred_element_type=jnp.fl...  70.9 us
    pmax x1, blocking collectives, local(): top = lax.pmax(row_top, 'src')  55.7 us
    gather x16, local copies, waits for them, and re-layouts, cols_of(): return col_part(rows_bf, f_rows, targets[ids], live)  54.9 us
    psum x1, blocking collectives, local(): total = lax.psum(row_total * jnp.exp(row_top - top), 'src')  52.9 us
    pmax x1, blocking collectives, local(): all_top = lax.pmax(tile_top, 'loop')  41.4 us
    all_gather x1, blocking collectives, plan_the_pairs_all(): return jnp.sum(lax.all_gather(block_in, 'loop'), axis=0)  34.2 us
    all_gather x1, blocking collectives, local(): ids_all = lax.all_gather(tile_ids[0], 'src')  21.4 us
  transfers between devices with their start and end apart: 1, of which 1 were waited for; matrix products, arithmetic and copies ran while one was open for 0% of the time, Pallas kernels for 0%

profile of v1, /device:TPU:0, one launch (start us, length us, event | category | flops | bytes accessed | tf_op | source)
XLA Modules:
  0.0 498.8 jit_solution(13316229181448420800)
XLA Ops:
  7.9 21.4 %all_gather.27 = s32[16,16,2]{1,2,0:T(2,128)S(1)} all-gather(s32[1,16,2]{1,2,0:T(2,128)} %param.16), channel_id=1, replica_groups=mesh['src'=16,'loop'=8] {'src'}, dimensions={0}, use_global_device_ids=true | all-gather | bytes 2176 | tf_op jit(solution)/shard_map/all_gather | solution.py:46
  30.1 17.0 %all-gather.4 = s32[16,1,16]{2,1,0:T(1,128)S(1)} all-gather(s32[1,1,16]{2,1,0:T(1,128)} %bitcast.89), channel_id=1, replica_groups=mesh['src'=16,'loop'=8] {'src'}, dimensions={0}, use_global_device_ids=true | all-gather | bytes 1088 | tf_op jit(solution)/shard_map/all_gather | solution.py:47
  47.5 18.6 %all-gather.3 = f32[16,1,512]{2,1,0:T(1,128)S(1)} all-gather(f32[1,1,512]{2,1,0:T(1,128)} %bitcast.87), channel_id=2, replica_groups=mesh['src'=16,'loop'=8] {'src'}, dimensions={0}, use_global_device_ids=true | all-gather | bytes 34816 | tf_op jit(solution)/shard_map/all_gather | solution.py:45
  66.2 18.0 %all-gather.7.cloned.1.call-done = bf16[8192,768]{1,0:T(8,128)(2,1)} async-done(((bf16[512,768]{1,0:T(8,128)(2,1)}), bf16[8192,768]{1,0:T(8,128)(2,1)}) %all-gather.7.cloned.1.call-update) | async-done | bytes 12582928 | tf_op jit(solution)/shard_map/all_gather | solution.py:44
  84.2 120.7 %while.24 = (s32[]{:T(128)}, f32[16,512]{1,0:T(8,128)S(1)}, f32[16,512]{1,0:T(8,128)S(1)}, pred[16,2]{1,0:T(8,128)(4,1)S(1)}, s32[16,2]{1,0:T(8,128)S(1)}, /*ind...) while((s32[]{:T(128)}, f32[16,512]{1,0:T(8,128)S(1)}, ...), condition=%wide.region_3.4_spmd, body=%wide.region_0.3_spmd.sunk | while | flops 808977408 | bytes 9732271 | solution.py:56
  85.5 3.4 gather_fusion
  93.1 3.4 gather_fusion
  100.6 3.4 gather_fusion
  108.1 3.4 gather_fusion
  115.7 3.4 gather_fusion
  123.2 3.4 gather_fusion
  130.8 3.4 gather_fusion
  138.3 3.4 gather_fusion
  145.9 3.4 gather_fusion
  153.4 3.4 gather_fusion
  161.0 3.4 gather_fusion
  168.5 3.4 gather_fusion
  176.1 3.4 gather_fusion
  204.9 55.7 %pmax.14 = f32[16,512]{1,0:T(8,128)S(1)} all-reduce(f32[16,512]{1,0:T(8,128)S(1)} %get-tuple-element.88), channel_id=1, replica_groups=mesh['src'=16,'loop'=8] {'src'}, use_global_device_ids=true, to_apply=%region_4.5 | all-reduce | flops 8192 | bytes 65536 | tf_op jit(solution)/shard_map/pmax | solution.py:57
  260.7 52.9 %psum.7 = f32[16,512]{1,0:T(8,128)S(1)} all-reduce(f32[16,512]{1,0:T(8,128)S(1)} %exponential_multiply_fusion), channel_id=1, replica_groups=mesh['src'=16,'loop'=8] {'src'}, use_global_device_ids=true, to_apply=%region_5.6 | all-reduce | flops 8192 | bytes 65536 | tf_op jit(solution)/shard_map/psum | solution.py:58
  314.2 101.2 %while.25 = (s32[]{:T(128)}, f32[16,2,512]{2,1,0:T(2,128)S(1)}, f32[16,2,512]{2,1,0:T(2,128)S(1)}, pred[16,2]{1,0:T(8,128)(4,1)S(1)}, f32[16,512]{1,0:T(8,128)S(...) while((s32[]{:T(128)}, f32[16,2,512]{2,1,0:T(2,128)S(1)}, ...), condition=%wide.region_9.10_spmd, body=%wide.region_6.9_spmd.sunk | while | flops 810025984 | bytes 9740957 | solution.py:66
  314.2 3.4 gather_fusion.2
  320.6 3.4 gather_fusion.2
  326.9 3.4 gather_fusion.2
  339.5 3.4 gather_fusion.2
  352.2 3.4 gather_fusion.2
  364.8 3.4 gather_fusion.2
  377.5 3.4 gather_fusion.2
  390.1 3.4 gather_fusion.2
  402.8 3.4 gather_fusion.2
  415.6 41.4 %pmax.15 = f32[8,512]{1,0:T(8,128)S(1)} all-reduce(f32[8,512]{1,0:T(8,128)S(1)} %select_reduce_fusion.1), channel_id=1, replica_groups=mesh['src'=16,'loop'=8] {'loop'}, use_global_device_ids=true, to_apply=%region_11.12 | all-reduce | flops 4096 | bytes 32768 | tf_op jit(solution)/shard_map/pmax | solution.py:76
  457.1 34.2 %all-gather.2 = f32[64,512]{1,0:T(8,128)S(1)} all-gather(f32[8,512]{1,0:T(8,128)S(1)} %exponential_multiply_fusion.1), channel_id=4, replica_groups=mesh['src'=16,'loop'=8] {'loop'}, dimensions={0}, use_global_device_ids=true | all-gather | bytes 147456 | tf_op jit(solution)/shard_map/all_gather | solution.py:12
  (292 shorter events, 148.3 us)
Async XLA Ops:
  7.2 77.0 %all-gather.7.cloned.1.call-start = ((), (), s32[]{:S(2)}) async-start(), calls=%async_computation | async-start | bytes 13369344 | tf_op jit(solution)/shard_map/all_gather | solution.py:44
  314.2 177.2 %copy-start = (f32[8,512]{1,0:T(8,128)S(1)}, f32[8,512]{1,0:T(8,128)}, u32[]{:S(2)}) copy-start(f32[8,512]{1,0:T(8,128)} %param.15) | copy-start | bytes 49156
Sparse Core Ops, SparseCore 0:
  9.7 74.4 all-gather.6
